TPU v7x, 128 devices: a whole 4x4x4 slice. The times are simulated.
128 devices in a mesh: freq: 8 (over z_hi, x), blk: 16 (over y, z_lo, core).
Axes of the slice: x: 4, y: 4, z: 4 (z_hi: 2, z_lo: 2; z = z_hi * 2 + z_lo), core: 2. Of those that a mesh axis runs over, the one named last changes fastest.
Arguments:
- traces: bfloat16 [2048, 2048, 256], P('blk', 'freq'), may hold values from -6 to 6
- signature: float32 [8, 2], P('freq'), may hold values from 0.5 to 1.5
Outputs:
- multiples: float32 [8, 2, 2048, 2048], P('freq', None, 'blk')
All inputs are finite; a program needn't handle non-finite values.
Results may differ from a plain program's by a relative error of at most 0.0035.
Values sent between devices are 32-bit elements; how exact they have to be, the bound alone decides.
No kernel may reach another device: no remote copies, remote signals or barrier semaphores. Data moves between devices by JAX's collectives and lax.ppermute only.
A program may use at most 256 MiB of HBM per device.

v0:
```python
import math
import jax
import jax.numpy as jnp
from jax import lax
from jax.sharding import PartitionSpec as P

BIN0 = 4
BINSTEP = 3
GROUP = 4


def make_table(freqs, samples):
    bins = BIN0 + BINSTEP * jnp.arange(freqs, dtype=jnp.int32)
    steps = jnp.arange(samples, dtype=jnp.int32)
    phase = steps[:, None] * bins[None, :] % samples
    angle = phase.astype(jnp.float32) * (2.0 * math.pi / samples)
    scale = 1.0 / math.sqrt(samples)
    table = jnp.concatenate([jnp.cos(angle) * scale, -jnp.sin(angle) * scale], axis=1)
    return table.astype(jnp.bfloat16)


def xor_perm(n, m):
    return [(i, i ^ m) for i in range(n)]


def shift_perm(n, s):
    return [(i, (i + s) % n) for i in range(n)]


def on_device(traces, signature):
    src_rows, rec_cols, samples = traces.shape
    freqs = lax.axis_size("freq")
    nblk = lax.axis_size("blk")
    ny = nblk // GROUP
    assert ny == 4 and nblk % GROUP == 0
    table = make_table(freqs, samples)
    projected = jnp.einsum("srt,tc->csr", traces, table, preferred_element_type=jnp.float32)
    projected = projected.reshape(2, freqs, src_rows, rec_cols)
    spectra = lax.all_to_all(projected, "freq", split_axis=1, concat_axis=3, tiled=True)
    own = spectra[:, 0]
    n = own.shape[2]
    rb = src_rows
    gw = GROUP * rb
    cw = n // GROUP
    b = lax.axis_index("blk")
    p = b % GROUP
    y = b // GROUP
    q1 = lax.ppermute(own, "blk", xor_perm(nblk, 1))
    q2 = lax.ppermute(own, "blk", xor_perm(nblk, 2))
    q3 = lax.ppermute(q2, "blk", xor_perm(nblk, 1))
    rows = jnp.concatenate([own, q1, q2, q3], axis=1)
    piece = lax.dynamic_slice_in_dim(rows, p * cw, cw, axis=2)
    l5 = rows.reshape(2, gw, ny, GROUP, rb)
    lx = jnp.concatenate(
        [lax.dynamic_slice_in_dim(l5, p ^ m, 1, axis=3) for m in range(GROUP)], axis=3
    ).reshape(2, gw, n)

    def contrib(g, pc, lo, hi):
        lg = lax.dynamic_slice_in_dim(lx, g * gw + lo * rb, (hi - lo) * rb, axis=2)
        return jnp.einsum(
            "aik,bkj->abij",
            lg,
            pc,
            precision=lax.Precision.HIGH,
            preferred_element_type=jnp.float32,
        )

    up = shift_perm(nblk, GROUP)
    dn = shift_perm(nblk, -GROUP)
    r_up = lax.ppermute(piece, "blk", up)
    r_dn = lax.ppermute(piece, "blk", dn)
    half = gw // 2
    f_up = lax.ppermute(r_up[:, :half], "blk", up)
    f_dn = lax.ppermute(r_dn[:, half:], "blk", dn)
    t = contrib(y, piece, 0, GROUP)
    t = t + contrib((y - 1) % ny, r_up, 0, GROUP)
    t = t + contrib((y + 1) % ny, r_dn, 0, GROUP)
    t = t + contrib((y + 2) % ny, f_up, 0, GROUP // 2)
    t = t + contrib((y + 2) % ny, f_dn, GROUP // 2, GROUP)
    prod_re = t[0, 0] - t[1, 1]
    prod_im = t[0, 1] + t[1, 0]
    scale = 1.0 / math.sqrt(n)
    w_re = signature[0, 0]
    w_im = signature[0, 1]
    out_re = -(w_re * prod_re - w_im * prod_im) * scale
    out_im = -(w_re * prod_im + w_im * prod_re) * scale
    blk_out = jnp.stack([out_re, out_im], axis=0)
    parts = [blk_out[:, :rb]]
    for m in range(1, GROUP):
        parts.append(lax.ppermute(blk_out[:, m * rb : (m + 1) * rb], "blk", xor_perm(nblk, m)))
    stacked = jnp.stack(parts, axis=0)
    ordered = [lax.dynamic_index_in_dim(stacked, p ^ i, 0, keepdims=False) for i in range(GROUP)]
    out = jnp.concatenate(ordered, axis=2)
    return out[None]


def solution(mesh):
    return jax.shard_map(
        on_device,
        mesh=mesh,
        in_specs=(P("blk", "freq", None), P("freq", None)),
        out_specs=P("freq", None, "blk", None),
        check_vma=False,
    )
```

profile of v0, /device:TPU:1, one launch (start us, length us, event | category | flops | bytes accessed | tf_op | source)
XLA Modules:
  0.0 226.6 jit_solution(9673138914343612404)
XLA Ops:
  0.1 10.2 %convolution_bitcast_fusion = f32[2,8,128,256]{3,1,0,2:T(8,128)S(1)} fusion(bf16[128,256,256]{2,1,0:T(8,128)(2,1)} %param.2, bf16[256,8]{0,1:T(8,128)(2,1)S(1)} %get-tuple-element.18, bf16[256,8]{0,1:T(8,128)(2,1)S(1)} %get-tuple-element.17), kind=kOutput, calls=%fused_computation.29 | convolution fusion | flops 268451840 | bytes 18882560 | tf_op jit(solution)/shard_map/srt,tc->csr/dot_general | solution.py:37
  11.5 35.7 %all_to_all.15 = f32[2,8,128,256]{3,0,2,1:T(2,128)} all-to-all(f32[2,8,128,256]{3,0,2,1:T(2,128)S(1)} %copy.44), channel_id=1, replica_groups=mesh['freq'=8,'blk'=16] {'freq'}, dimensions={1} | all-to-all | bytes 4194304 | tf_op jit(solution)/shard_map/all_to_all | solution.py:39
  47.2 2.7 %copy.45 = f32[2,8,128,256]{2,3,1,0:T(8,128)S(1)} copy(f32[2,8,128,256]{3,0,2,1:T(2,128)} %all_to_all.15) | data formatting | bytes 4194304 | tf_op jit(solution)/shard_map/all_to_all | solution.py:39
  50.7 2.0 collective-permute-start
  52.8 42.8 %collective-permute-done.1 = f32[2,128,2048]{1,2,0:T(8,128)} collective-permute-done((f32[2,128,2048]{1,2,0:T(8,128)S(1)}, f32[2,128,2048]{1,2,0:T(8,128)}, u32[]{:S(2)}, u32[]{:S(2)}) %collective-permute-start.1) | collective-permute-done | bytes 2097184 | tf_op jit(solution)/shard_map/ppermute | solution.py:49
  95.5 2.6 %collective-permute-start.2 = (f32[2,128,2048]{1,2,0:T(8,128)}, f32[2,128,2048]{1,2,0:T(8,128)}, u32[]{:S(2)}, u32[]{:S(2)}) collective-permute-start(f32[2,128,2048]{1,2,0:T(8,128)} %collective-permute-done.1), channel_id=1, source_target_pairs={{0,1},{1,0},{2,3},{3,2},{4,5},{5,4},{6,7},{7,6},{8,9},{9,8},{10,11... | collective-permute-start | bytes 6291464 | tf_op jit(solution)/shard_map/ppermute | solution.py:50
  98.1 4.1 %collective-permute-done.2 = f32[2,128,2048]{1,2,0:T(8,128)} collective-permute-done((f32[2,128,2048]{1,2,0:T(8,128)}, f32[2,128,2048]{1,2,0:T(8,128)}, u32[]{:S(2)}, u32[]{:S(2)}) %collective-permute-start.2) | collective-permute-done | bytes 2097184 | tf_op jit(solution)/shard_map/ppermute | solution.py:50
  102.3 2.8 %fusion.2 = f32[2,512,512]{1,2,0:T(8,128)} fusion(s32[]{:T(128)S(6)} %select_n.70, f32[2,128,2048]{1,2,0:T(8,128)S(1)} %bitcast.124, f32[2,128,2048]{1,2,0:T(8,128)} %collective-permute-done, f32[2,128,2048]{1,2,0:T(8,128)} %collective-permute-done.1, f32[2,128,2048]{1,2,0:T(8,128)} %collective-permute-done.2), kind=kLoop, calls=%fused_computation.15 | loop fusion | flops 1572864 | bytes 10485764 | tf_op jit(solution)/shard_map/concatenate | solution.py:51
  108.4 3.1 %pad_maximum_fusion = f32[2,512,4,4,128]{1,4,3,2,0:T(8,128)S(1)} fusion(f32[2,128,4,4,128]{1,4,3,2,0:T(8,128)} %bitcast.13, f32[2,128,4,4,128]{1,4,3,2,0:T(8,128)} %bitcast.12, f32[2,128,4,4,128]{1,4,3,2,0:T(8,128)} %bitcast.11, f32[2,128,4,4,128]{1,4,3,2,0:T(8,128)S(1)} %bitcast.125), kind=kLoop, calls=%fused_computation.4 | loop fusion | flops 6291456 | bytes 16777216 | tf_op jit(solution)/shard_map/concatenate | solution.py:51
  111.6 1.6 constant_dynamic-slice_fusion.7
  113.2 40.4 %collective-permute-done.3 = f32[2,512,512]{1,2,0:T(8,128)} collective-permute-done((f32[2,512,512]{1,2,0:T(8,128)}, f32[2,512,512]{1,2,0:T(8,128)}, u32[]{:S(2)}, u32[]{:S(2)}) %collective-permute-start.3) | collective-permute-done | bytes 2097184 | tf_op jit(solution)/shard_map/ppermute | solution.py:70
  157.5 2.9 %collective-permute-start.6 = (f32[2,256,512]{1,2,0:T(8,128)S(1)}, f32[2,256,512]{1,2,0:T(8,128)S(1)}, u32[]{:S(2)}, u32[]{:S(2)}) collective-permute-start(f32[2,256,512]{1,2,0:T(8,128)S(1)} %slice.49), channel_id=1, source_target_pairs={{0,12},{1,13},{2,14},{3,15},{4,0},{5,1},{6,2},{7,3},{8,4},{9,5},{1... | collective-permute-start | bytes 3145736 | tf_op jit(solution)/shard_map/ppermute | solution.py:74
  160.4 5.1 %fusion.5 = f32[2,512,2,512]{3,1,2,0:T(8,128)S(1)} fusion(f32[2,512,512]{1,2,0:T(8,128)} %collective-permute-done.3, f32[2,512,2048]{1,2,0:T(8,128)S(1)} %bitcast.117, s32[]{:T(128)S(6)} %select_n.78), kind=kOutput, calls=%fused_computation.20 | convolution fusion | flops 3221225472 | bytes 8388612 | tf_op jit(solution)/shard_map/aik,bkj->abij/dot_general | solution.py:60
  165.5 5.1 %fusion.3 = f32[2,512,2,512]{3,1,2,0:T(8,128)S(1)} fusion(f32[2,512,512]{1,2,0:T(8,128)} %collective-permute-done.4, f32[2,512,2048]{1,2,0:T(8,128)S(1)} %bitcast.118, s32[]{:T(128)S(6)} %select_n.80), kind=kOutput, calls=%fused_computation.18 | convolution fusion | flops 3221225472 | bytes 8388612 | tf_op jit(solution)/shard_map/aik,bkj->abij/dot_general | solution.py:60
  170.5 9.1 %collective-permute-done.5 = f32[2,256,512]{1,2,0:T(8,128)S(1)} collective-permute-done((f32[2,256,512]{1,2,0:T(8,128)S(1)}, f32[2,256,512]{1,2,0:T(8,128)S(1)}, u32[]{:S(2)}, u32[]{:S(2)}) %collective-permute-start.5) | collective-permute-done | bytes 1048608 | tf_op jit(solution)/shard_map/ppermute | solution.py:73
  179.7 1.8 fusion.17
  181.5 3.8 %fusion.15 = f32[2,512,2,512]{3,1,2,0:T(8,128)} fusion(f32[2,256,512]{1,2,0:T(8,128)S(1)} %collective-permute-done.6, f32[2,512,2048]{1,2,0:T(8,128)S(1)} %bitcast.120, s32[]{:T(128)S(6)} %select_n.83), kind=kOutput, calls=%fused_computation.34 | convolution fusion | flops 1610612736 | bytes 6291460 | tf_op jit(solution)/shard_map/aik,bkj->abij/dot_general | solution.py:60
  185.3 7.7 %add_bitcast_fusion = f32[2,2,512,512]{2,3,0,1:T(8,128)S(1)} fusion(f32[2,512,2,512]{3,1,2,0:T(8,128)} %fusion.15, f32[2,512,2,512]{3,1,2,0:T(8,128)S(1)} %fusion.17, f32[2,512,2,512]{3,1,2,0:T(8,128)S(1)} %fusion.3, f32[2,512,2,512]{3,1,2,0:T(8,128)S(1)} %fusion.5, f32[2,512,512]{1,2,0:T(8,128)} %fusion.2, f32[2,512,2048]{1,2,0:T(8,128)S(1)} %bitcast.121, ...), kind=kOutput, calls=%fused_computation.6 | convolution fusion | flops 3225419776 | bytes 25165828 | tf_op jit(solution)/shard_map/aik,bkj->abij/dot_general | solution.py:60
  193.0 1.8 fusion.23
  194.8 1.8 fusion.27
  196.8 2.3 %collective-permute-start.7 = (f32[2,128,512]{1,2,0:T(8,128)S(1)}, f32[2,128,512]{1,2,0:T(8,128)S(1)}, u32[]{:S(2)}, u32[]{:S(2)}) collective-permute-start(f32[2,128,512]{1,2,0:T(8,128)S(1)} %get-tuple-element.14), channel_id=1, source_target_pairs={{0,1},{1,0},{2,3},{3,2},{4,5},{5,4},{6,7},{7,6},{8,9},{9,8},{10,11... | collective-permute-start | bytes 1572872 | tf_op jit(solution)/shard_map/ppermute | solution.py:90
  200.8 11.7 %collective-permute-done.8 = f32[2,128,512]{1,2,0:T(8,128)S(1)} collective-permute-done((f32[2,128,512]{1,2,0:T(8,128)S(1)}, f32[2,128,512]{1,2,0:T(8,128)S(1)}, u32[]{:S(2)}, u32[]{:S(2)}) %collective-permute-start.8) | collective-permute-done | bytes 524320 | tf_op jit(solution)/shard_map/ppermute | solution.py:90
  212.5 11.5 %collective-permute-done.9 = f32[2,128,512]{1,2,0:T(8,128)S(1)} collective-permute-done((f32[2,128,512]{1,2,0:T(8,128)S(1)}, f32[2,128,512]{1,2,0:T(8,128)S(1)}, u32[]{:S(2)}, u32[]{:S(2)}) %collective-permute-start.9) | collective-permute-done | bytes 524320 | tf_op jit(solution)/shard_map/ppermute | solution.py:90
  225.1 1.5 maximum_bitcast_fusion
  (26 shorter events, 12.3 us)
Async XLA Ops:
  49.9 45.6 %collective-permute-start.1 = (f32[2,128,2048]{1,2,0:T(8,128)S(1)}, f32[2,128,2048]{1,2,0:T(8,128)}, u32[]{:S(2)}, u32[]{:S(2)}) collective-permute-start(f32[2,128,2048]{1,2,0:T(8,128)S(1)} %bitcast.122), channel_id=1, source_target_pairs={{0,2},{1,3},{2,0},{3,1},{4,6},{5,7},{6,4},{7,5},{8,10},{9,11},{10,... | collective-permute-start | bytes 6291464 | tf_op jit(solution)/shard_map/ppermute | solution.py:49
  50.7 47.4 %collective-permute-start = (f32[2,128,2048]{1,2,0:T(8,128)S(1)}, f32[2,128,2048]{1,2,0:T(8,128)}, u32[]{:S(2)}, u32[]{:S(2)}) collective-permute-start(f32[2,128,2048]{1,2,0:T(8,128)S(1)} %bitcast.123), channel_id=1, source_target_pairs={{0,1},{1,0},{2,3},{3,2},{4,5},{5,4},{6,7},{7,6},{8,9},{9,8},{10,11... | collective-permute-start | bytes 6291464 | tf_op jit(solution)/shard_map/ppermute | solution.py:48
  95.5 6.7 %collective-permute-start.2 = (f32[2,128,2048]{1,2,0:T(8,128)}, f32[2,128,2048]{1,2,0:T(8,128)}, u32[]{:S(2)}, u32[]{:S(2)}) collective-permute-start(f32[2,128,2048]{1,2,0:T(8,128)} %collective-permute-done.1), channel_id=1, source_target_pairs={{0,1},{1,0},{2,3},{3,2},{4,5},{5,4},{6,7},{7,6},{8,9},{9,8},{10,11... | collective-permute-start | bytes 6291464 | tf_op jit(solution)/shard_map/ppermute | solution.py:50
  98.1 9.7 %copy-start = (f32[1,2]{1,0:T(1,128)S(1)}, f32[1,2]{1,0:T(1,128)}, u32[]{:S(2)}) copy-start(f32[1,2]{1,0:T(1,128)} %param.3) | copy-start | bytes 28
  105.1 48.5 %collective-permute-start.3 = (f32[2,512,512]{1,2,0:T(8,128)}, f32[2,512,512]{1,2,0:T(8,128)}, u32[]{:S(2)}, u32[]{:S(2)}) collective-permute-start(f32[2,512,512]{1,2,0:T(8,128)} %fusion.2), channel_id=1, source_target_pairs={{0,4},{1,5},{2,6},{3,7},{4,8},{5,9},{6,10},{7,11},{8,12},{9,13},{1... | collective-permute-start | bytes 6291464 | tf_op jit(solution)/shard_map/ppermute | solution.py:70
  106.4 49.8 %collective-permute-start.4 = (f32[2,512,512]{1,2,0:T(8,128)}, f32[2,512,512]{1,2,0:T(8,128)}, u32[]{:S(2)}, u32[]{:S(2)}) collective-permute-start(f32[2,512,512]{1,2,0:T(8,128)} %fusion.2), channel_id=1, source_target_pairs={{0,12},{1,13},{2,14},{3,15},{4,0},{5,1},{6,2},{7,3},{8,4},{9,5},{1... | collective-permute-start | bytes 6291464 | tf_op jit(solution)/shard_map/ppermute | solution.py:71
  154.8 24.8 %collective-permute-start.5 = (f32[2,256,512]{1,2,0:T(8,128)S(1)}, f32[2,256,512]{1,2,0:T(8,128)S(1)}, u32[]{:S(2)}, u32[]{:S(2)}) collective-permute-start(f32[2,256,512]{1,2,0:T(8,128)S(1)} %slice.48), channel_id=1, source_target_pairs={{0,4},{1,5},{2,6},{3,7},{4,8},{5,9},{6,10},{7,11},{8,12},{9,13},{1... | collective-permute-start | bytes 3145736 | tf_op jit(solution)/shard_map/ppermute | solution.py:73
  157.5 24.0 %collective-permute-start.6 = (f32[2,256,512]{1,2,0:T(8,128)S(1)}, f32[2,256,512]{1,2,0:T(8,128)S(1)}, u32[]{:S(2)}, u32[]{:S(2)}) collective-permute-start(f32[2,256,512]{1,2,0:T(8,128)S(1)} %slice.49), channel_id=1, source_target_pairs={{0,12},{1,13},{2,14},{3,15},{4,0},{5,1},{6,2},{7,3},{8,4},{9,5},{1... | collective-permute-start | bytes 3145736 | tf_op jit(solution)/shard_map/ppermute | solution.py:74
  196.8 4.0 %collective-permute-start.7 = (f32[2,128,512]{1,2,0:T(8,128)S(1)}, f32[2,128,512]{1,2,0:T(8,128)S(1)}, u32[]{:S(2)}, u32[]{:S(2)}) collective-permute-start(f32[2,128,512]{1,2,0:T(8,128)S(1)} %get-tuple-element.14), channel_id=1, source_target_pairs={{0,1},{1,0},{2,3},{3,2},{4,5},{5,4},{6,7},{7,6},{8,9},{9,8},{10,11... | collective-permute-start | bytes 1572872 | tf_op jit(solution)/shard_map/ppermute | solution.py:90
  199.1 13.4 %collective-permute-start.8 = (f32[2,128,512]{1,2,0:T(8,128)S(1)}, f32[2,128,512]{1,2,0:T(8,128)S(1)}, u32[]{:S(2)}, u32[]{:S(2)}) collective-permute-start(f32[2,128,512]{1,2,0:T(8,128)S(1)} %get-tuple-element.16), channel_id=1, source_target_pairs={{0,2},{1,3},{2,0},{3,1},{4,6},{5,7},{6,4},{7,5},{8,10},{9,11},{10,... | collective-permute-start | bytes 1572872 | tf_op jit(solution)/shard_map/ppermute | solution.py:90
  199.8 24.1 %collective-permute-start.9 = (f32[2,128,512]{1,2,0:T(8,128)S(1)}, f32[2,128,512]{1,2,0:T(8,128)S(1)}, u32[]{:S(2)}, u32[]{:S(2)}) collective-permute-start(f32[2,128,512]{1,2,0:T(8,128)S(1)} %get-tuple-element.15), channel_id=1, source_target_pairs={{0,3},{1,2},{2,1},{3,0},{4,7},{5,6},{6,5},{7,4},{8,11},{9,10},{10,... | collective-permute-start | bytes 1572872 | tf_op jit(solution)/shard_map/ppermute | solution.py:90
where the time goes:
time: 227 us
  waiting for transfers between devices  120 us (53%)
  blocking collectives  35.7 us (16%)
  matrix products  33.6 us (15%)
  starting transfers between devices  15.2 us (7%)
  other arithmetic  12.8 us (6%)
  local copies, waits for them, and re-layouts  9.57 us (4%)
    ppermute x1, waiting for transfers between devices, on_device(): q2 = lax.ppermute(own, 'blk', xor_perm(nblk, 2))  42.8 us
    ppermute x1, waiting for transfers between devices, on_device(): r_up = lax.ppermute(piece, 'blk', up)  40.4 us
    all_to_all x1, blocking collectives, on_device(): lax.all_to_all(projected, 'freq', split_axis=1, concat_axis=3, tiled=True)  35.7 us
    dot_general x5, matrix products, contrib(): jnp.einsum('aik,bkj->abij', lg, pc, precision=lax.Precision.HIGH, preferr...  23.4 us
    ppermute x3, waiting for transfers between devices, on_device(): lax.ppermute(blk_out[:, m * rb:(m + 1) * rb], 'blk', xor_perm(nblk, m))  23.2 us
    dot_general x1, matrix products, on_device(): jnp.einsum('srt,tc->csr', traces, table, preferred_element_type=jnp.float32)  10.2 us
    ppermute x1, waiting for transfers between devices, on_device(): f_up = lax.ppermute(r_up[:, :half], 'blk', up)  9.13 us
    concatenate x2, other arithmetic, on_device(): rows = jnp.concatenate([own, q1, q2, q3], axis=1)  5.96 us
  transfers between devices with their start and end apart: 10, of which 6 were waited for; matrix products, arithmetic and copies ran while one was open for 9% of the time, Pallas kernels for 0%

commit v1 on v0

--- a/solution.py
+++ b/solution.py
@@ -36,7 +36,13 @@
     table = make_table(freqs, samples)
     projected = jnp.einsum("srt,tc->csr", traces, table, preferred_element_type=jnp.float32)
     projected = projected.reshape(2, freqs, src_rows, rec_cols)
-    spectra = lax.all_to_all(projected, "freq", split_axis=1, concat_axis=3, tiled=True)
+    mix_bands = lambda array_here, d_out, array_dim: jnp.concatenate(
+        lax.all_to_all(
+            jnp.stack(jnp.split(array_here, lax.axis_size("freq"), d_out), 0), "freq", 0, 0
+        ),
+        axis=array_dim,
+    )
+    spectra = mix_bands(projected, 1, 3)
     own = spectra[:, 0]
     n = own.shape[2]
     rb = src_rows

time: 227 us -> 237 us (1.044)
  local copies, waits for them, and re-layouts: 9.57 us -> 19 us
    unnamed x2 -> x17, local copies, waits for them, and re-layouts: 0.01 us -> 10.9 us
    all_to_all x1, local copies, waits for them, and re-layouts: 2.73 us -> 0.14 us  [on_device(): lax.all_to_all(jnp.stack(jnp.split(array_here, lax.axis_size('freq'), d_o...]
where the time goes in v1:
time: 237 us; the launch traced here: 236 us
  waiting for transfers between devices  120 us (51%)
  blocking collectives  35.6 us (15%)
  matrix products  33.6 us (14%)
  local copies, waits for them, and re-layouts  19 us (8%)
  starting transfers between devices  15.2 us (6%)
  other arithmetic  12.8 us (5%)
    ppermute x1, waiting for transfers between devices, on_device(): q2 = lax.ppermute(own, 'blk', xor_perm(nblk, 2))  42.8 us
    ppermute x1, waiting for transfers between devices, on_device(): r_up = lax.ppermute(piece, 'blk', up)  40.3 us
    all_to_all x1, blocking collectives, on_device(): lax.all_to_all(jnp.stack(jnp.split(array_here, lax.axis_size('freq'), d_o...  35.6 us
    dot_general x5, matrix products, contrib(): jnp.einsum('aik,bkj->abij', lg, pc, precision=lax.Precision.HIGH, preferr...  23.4 us
    ppermute x3, waiting for transfers between devices, on_device(): lax.ppermute(blk_out[:, m * rb:(m + 1) * rb], 'blk', xor_perm(nblk, m))  23.2 us
    unnamed x17, local copies, waits for them, and re-layouts  10.9 us
    dot_general x1, matrix products, on_device(): jnp.einsum('srt,tc->csr', traces, table, preferred_element_type=jnp.float32)  10.2 us
    ppermute x1, waiting for transfers between devices, on_device(): f_up = lax.ppermute(r_up[:, :half], 'blk', up)  9.13 us
  transfers between devices with their start and end apart: 10, of which 6 were waited for; matrix products, arithmetic and copies ran while one was open for 9% of the time, Pallas kernels for 0%

profile of v1, /device:TPU:1, one launch (start us, length us, event | category | flops | bytes accessed | tf_op | source)
XLA Modules:
  0.0 236.0 jit_solution(2262338947830233752)
XLA Ops:
  0.1 10.2 %convolution_bitcast_fusion = f32[2,8,128,256]{3,1,0,2:T(8,128)S(1)} fusion(bf16[128,256,256]{2,1,0:T(8,128)(2,1)} %param.2, bf16[256,8]{0,1:T(8,128)(2,1)S(1)} %get-tuple-element.26, bf16[256,8]{0,1:T(8,128)(2,1)S(1)} %get-tuple-element.25), kind=kOutput, calls=%fused_computation.29 | convolution fusion | flops 268451840 | bytes 18882560 | tf_op jit(solution)/shard_map/srt,tc->csr/dot_general | solution.py:37
  10.4 2.2 fusion.48
  12.6 1.8 copy.65
  15.3 1.8 copy.66
  23.5 35.6 %all_to_all.5 = f32[8,2,1,128,256]{3,4,1,2,0:T(8,128)S(1)} all-to-all(f32[8,2,1,128,256]{3,4,1,2,0:T(8,128)S(1)} %bitcast_dynamic-update-slice_fusion), channel_id=1, replica_groups=mesh['freq'=8,'blk'=16] {'freq'}, dimensions={0} | all-to-all | bytes 4194304 | tf_op jit(solution)/shard_map/all_to_all | solution.py:40
  60.1 2.0 collective-permute-start
  62.1 42.8 %collective-permute-done.1 = f32[2,128,2048]{1,2,0:T(8,128)} collective-permute-done((f32[2,128,2048]{1,2,0:T(8,128)S(1)}, f32[2,128,2048]{1,2,0:T(8,128)}, u32[]{:S(2)}, u32[]{:S(2)}) %collective-permute-start.1) | collective-permute-done | bytes 2097184 | tf_op jit(solution)/shard_map/ppermute | solution.py:55
  104.9 2.6 %collective-permute-start.2 = (f32[2,128,2048]{1,2,0:T(8,128)}, f32[2,128,2048]{1,2,0:T(8,128)}, u32[]{:S(2)}, u32[]{:S(2)}) collective-permute-start(f32[2,128,2048]{1,2,0:T(8,128)} %collective-permute-done.1), channel_id=1, source_target_pairs={{0,1},{1,0},{2,3},{3,2},{4,5},{5,4},{6,7},{7,6},{8,9},{9,8},{10,11... | collective-permute-start | bytes 6291464 | tf_op jit(solution)/shard_map/ppermute | solution.py:56
  107.5 4.1 %collective-permute-done.2 = f32[2,128,2048]{1,2,0:T(8,128)} collective-permute-done((f32[2,128,2048]{1,2,0:T(8,128)}, f32[2,128,2048]{1,2,0:T(8,128)}, u32[]{:S(2)}, u32[]{:S(2)}) %collective-permute-start.2) | collective-permute-done | bytes 2097184 | tf_op jit(solution)/shard_map/ppermute | solution.py:56
  111.6 2.8 %fusion.2 = f32[2,512,512]{1,2,0:T(8,128)} fusion(s32[]{:T(128)S(6)} %select_n.70, f32[2,128,2048]{1,2,0:T(8,128)S(1)} %bitcast.138, f32[2,128,2048]{1,2,0:T(8,128)} %collective-permute-done, f32[2,128,2048]{1,2,0:T(8,128)} %collective-permute-done.1, f32[2,128,2048]{1,2,0:T(8,128)} %collective-permute-done.2), kind=kLoop, calls=%fused_computation.15 | loop fusion | flops 1572864 | bytes 10485764 | tf_op jit(solution)/shard_map/concatenate | solution.py:57
  117.8 3.1 %pad_maximum_fusion = f32[2,512,4,4,128]{1,4,3,2,0:T(8,128)S(1)} fusion(f32[2,128,4,4,128]{1,4,3,2,0:T(8,128)} %bitcast.19, f32[2,128,4,4,128]{1,4,3,2,0:T(8,128)} %bitcast.18, f32[2,128,4,4,128]{1,4,3,2,0:T(8,128)} %bitcast.17, f32[2,128,4,4,128]{1,4,3,2,0:T(8,128)S(1)} %bitcast.139), kind=kLoop, calls=%fused_computation.4 | loop fusion | flops 6291456 | bytes 16777216 | tf_op jit(solution)/shard_map/concatenate | solution.py:57
  122.6 40.3 %collective-permute-done.3 = f32[2,512,512]{1,2,0:T(8,128)} collective-permute-done((f32[2,512,512]{1,2,0:T(8,128)}, f32[2,512,512]{1,2,0:T(8,128)}, u32[]{:S(2)}, u32[]{:S(2)}) %collective-permute-start.3) | collective-permute-done | bytes 2097184 | tf_op jit(solution)/shard_map/ppermute | solution.py:76
  166.9 2.9 %collective-permute-start.6 = (f32[2,256,512]{1,2,0:T(8,128)S(1)}, f32[2,256,512]{1,2,0:T(8,128)S(1)}, u32[]{:S(2)}, u32[]{:S(2)}) collective-permute-start(f32[2,256,512]{1,2,0:T(8,128)S(1)} %slice.49), channel_id=1, source_target_pairs={{0,12},{1,13},{2,14},{3,15},{4,0},{5,1},{6,2},{7,3},{8,4},{9,5},{1... | collective-permute-start | bytes 3145736 | tf_op jit(solution)/shard_map/ppermute | solution.py:80
  169.7 5.1 %fusion.5 = f32[2,512,2,512]{3,1,2,0:T(8,128)S(1)} fusion(f32[2,512,512]{1,2,0:T(8,128)} %collective-permute-done.3, f32[2,512,2048]{1,2,0:T(8,128)S(1)} %bitcast.131, s32[]{:T(128)S(6)} %select_n.78), kind=kOutput, calls=%fused_computation.20 | convolution fusion | flops 3221225472 | bytes 8388612 | tf_op jit(solution)/shard_map/aik,bkj->abij/dot_general | solution.py:66
  174.8 5.1 %fusion.3 = f32[2,512,2,512]{3,1,2,0:T(8,128)S(1)} fusion(f32[2,512,512]{1,2,0:T(8,128)} %collective-permute-done.4, f32[2,512,2048]{1,2,0:T(8,128)S(1)} %bitcast.132, s32[]{:T(128)S(6)} %select_n.80), kind=kOutput, calls=%fused_computation.18 | convolution fusion | flops 3221225472 | bytes 8388612 | tf_op jit(solution)/shard_map/aik,bkj->abij/dot_general | solution.py:66
  179.9 9.1 %collective-permute-done.5 = f32[2,256,512]{1,2,0:T(8,128)S(1)} collective-permute-done((f32[2,256,512]{1,2,0:T(8,128)S(1)}, f32[2,256,512]{1,2,0:T(8,128)S(1)}, u32[]{:S(2)}, u32[]{:S(2)}) %collective-permute-start.5) | collective-permute-done | bytes 1048608 | tf_op jit(solution)/shard_map/ppermute | solution.py:79
  189.0 1.8 fusion.17
  190.9 3.8 %fusion.15 = f32[2,512,2,512]{3,1,2,0:T(8,128)} fusion(f32[2,256,512]{1,2,0:T(8,128)S(1)} %collective-permute-done.6, f32[2,512,2048]{1,2,0:T(8,128)S(1)} %bitcast.134, s32[]{:T(128)S(6)} %select_n.83), kind=kOutput, calls=%fused_computation.34 | convolution fusion | flops 1610612736 | bytes 6291460 | tf_op jit(solution)/shard_map/aik,bkj->abij/dot_general | solution.py:66
  194.7 7.7 %add_bitcast_fusion = f32[2,2,512,512]{2,3,0,1:T(8,128)S(1)} fusion(f32[2,512,2,512]{3,1,2,0:T(8,128)} %fusion.15, f32[2,512,2,512]{3,1,2,0:T(8,128)S(1)} %fusion.17, f32[2,512,2,512]{3,1,2,0:T(8,128)S(1)} %fusion.3, f32[2,512,2,512]{3,1,2,0:T(8,128)S(1)} %fusion.5, f32[2,512,512]{1,2,0:T(8,128)} %fusion.2, f32[2,512,2048]{1,2,0:T(8,128)S(1)} %bitcast.135, ...), kind=kOutput, calls=%fused_computation.6 | convolution fusion | flops 3225419776 | bytes 25165828 | tf_op jit(solution)/shard_map/aik,bkj->abij/dot_general | solution.py:66
  202.3 1.8 fusion.23
  204.2 1.8 fusion.27
  206.1 2.3 collective-permute-start.7
  210.2 11.7 %collective-permute-done.8 = f32[2,128,512]{1,2,0:T(8,128)S(1)} collective-permute-done((f32[2,128,512]{1,2,0:T(8,128)S(1)}, f32[2,128,512]{1,2,0:T(8,128)S(1)}, u32[]{:S(2)}, u32[]{:S(2)}) %collective-permute-start.8) | collective-permute-done | bytes 524320 | tf_op jit(solution)/shard_map/ppermute | solution.py:96
  221.8 11.5 %collective-permute-done.9 = f32[2,128,512]{1,2,0:T(8,128)S(1)} collective-permute-done((f32[2,128,512]{1,2,0:T(8,128)S(1)}, f32[2,128,512]{1,2,0:T(8,128)S(1)}, u32[]{:S(2)}, u32[]{:S(2)}) %collective-permute-start.9) | collective-permute-done | bytes 524320 | tf_op jit(solution)/shard_map/ppermute | solution.py:96
  (42 shorter events, 21.8 us)
Async XLA Ops:
  59.3 45.6 %collective-permute-start.1 = (f32[2,128,2048]{1,2,0:T(8,128)S(1)}, f32[2,128,2048]{1,2,0:T(8,128)}, u32[]{:S(2)}, u32[]{:S(2)}) collective-permute-start(f32[2,128,2048]{1,2,0:T(8,128)S(1)} %bitcast.136), channel_id=1, source_target_pairs={{0,2},{1,3},{2,0},{3,1},{4,6},{5,7},{6,4},{7,5},{8,10},{9,11},{10,... | collective-permute-start | bytes 6291464 | tf_op jit(solution)/shard_map/ppermute | solution.py:55
  60.1 47.4 %collective-permute-start = (f32[2,128,2048]{1,2,0:T(8,128)S(1)}, f32[2,128,2048]{1,2,0:T(8,128)}, u32[]{:S(2)}, u32[]{:S(2)}) collective-permute-start(f32[2,128,2048]{1,2,0:T(8,128)S(1)} %bitcast.137), channel_id=1, source_target_pairs={{0,1},{1,0},{2,3},{3,2},{4,5},{5,4},{6,7},{7,6},{8,9},{9,8},{10,11... | collective-permute-start | bytes 6291464 | tf_op jit(solution)/shard_map/ppermute | solution.py:54
  104.9 6.7 %collective-permute-start.2 = (f32[2,128,2048]{1,2,0:T(8,128)}, f32[2,128,2048]{1,2,0:T(8,128)}, u32[]{:S(2)}, u32[]{:S(2)}) collective-permute-start(f32[2,128,2048]{1,2,0:T(8,128)} %collective-permute-done.1), channel_id=1, source_target_pairs={{0,1},{1,0},{2,3},{3,2},{4,5},{5,4},{6,7},{7,6},{8,9},{9,8},{10,11... | collective-permute-start | bytes 6291464 | tf_op jit(solution)/shard_map/ppermute | solution.py:56
  107.5 9.7 %copy-start = (f32[1,2]{1,0:T(1,128)S(1)}, f32[1,2]{1,0:T(1,128)}, u32[]{:S(2)}) copy-start(f32[1,2]{1,0:T(1,128)} %param.3) | copy-start | bytes 28
  114.5 48.5 %collective-permute-start.3 = (f32[2,512,512]{1,2,0:T(8,128)}, f32[2,512,512]{1,2,0:T(8,128)}, u32[]{:S(2)}, u32[]{:S(2)}) collective-permute-start(f32[2,512,512]{1,2,0:T(8,128)} %fusion.2), channel_id=1, source_target_pairs={{0,4},{1,5},{2,6},{3,7},{4,8},{5,9},{6,10},{7,11},{8,12},{9,13},{1... | collective-permute-start | bytes 6291464 | tf_op jit(solution)/shard_map/ppermute | solution.py:76
  115.8 49.8 %collective-permute-start.4 = (f32[2,512,512]{1,2,0:T(8,128)}, f32[2,512,512]{1,2,0:T(8,128)}, u32[]{:S(2)}, u32[]{:S(2)}) collective-permute-start(f32[2,512,512]{1,2,0:T(8,128)} %fusion.2), channel_id=1, source_target_pairs={{0,12},{1,13},{2,14},{3,15},{4,0},{5,1},{6,2},{7,3},{8,4},{9,5},{1... | collective-permute-start | bytes 6291464 | tf_op jit(solution)/shard_map/ppermute | solution.py:77
  164.2 24.8 %collective-permute-start.5 = (f32[2,256,512]{1,2,0:T(8,128)S(1)}, f32[2,256,512]{1,2,0:T(8,128)S(1)}, u32[]{:S(2)}, u32[]{:S(2)}) collective-permute-start(f32[2,256,512]{1,2,0:T(8,128)S(1)} %slice.48), channel_id=1, source_target_pairs={{0,4},{1,5},{2,6},{3,7},{4,8},{5,9},{6,10},{7,11},{8,12},{9,13},{1... | collective-permute-start | bytes 3145736 | tf_op jit(solution)/shard_map/ppermute | solution.py:79
  166.9 24.0 %collective-permute-start.6 = (f32[2,256,512]{1,2,0:T(8,128)S(1)}, f32[2,256,512]{1,2,0:T(8,128)S(1)}, u32[]{:S(2)}, u32[]{:S(2)}) collective-permute-start(f32[2,256,512]{1,2,0:T(8,128)S(1)} %slice.49), channel_id=1, source_target_pairs={{0,12},{1,13},{2,14},{3,15},{4,0},{5,1},{6,2},{7,3},{8,4},{9,5},{1... | collective-permute-start | bytes 3145736 | tf_op jit(solution)/shard_map/ppermute | solution.py:80
  206.1 4.1 %collective-permute-start.7 = (f32[2,128,512]{1,2,0:T(8,128)S(1)}, f32[2,128,512]{1,2,0:T(8,128)S(1)}, u32[]{:S(2)}, u32[]{:S(2)}) collective-permute-start(f32[2,128,512]{1,2,0:T(8,128)S(1)} %get-tuple-element.14), channel_id=1, source_target_pairs={{0,1},{1,0},{2,3},{3,2},{4,5},{5,4},{6,7},{7,6},{8,9},{9,8},{10,11... | collective-permute-start | bytes 1572872 | tf_op jit(solution)/shard_map/ppermute | solution.py:96
  208.4 13.4 %collective-permute-start.8 = (f32[2,128,512]{1,2,0:T(8,128)S(1)}, f32[2,128,512]{1,2,0:T(8,128)S(1)}, u32[]{:S(2)}, u32[]{:S(2)}) collective-permute-start(f32[2,128,512]{1,2,0:T(8,128)S(1)} %get-tuple-element.16), channel_id=1, source_target_pairs={{0,2},{1,3},{2,0},{3,1},{4,6},{5,7},{6,4},{7,5},{8,10},{9,11},{10,... | collective-permute-start | bytes 1572872 | tf_op jit(solution)/shard_map/ppermute | solution.py:96
  209.2 24.1 %collective-permute-start.9 = (f32[2,128,512]{1,2,0:T(8,128)S(1)}, f32[2,128,512]{1,2,0:T(8,128)S(1)}, u32[]{:S(2)}, u32[]{:S(2)}) collective-permute-start(f32[2,128,512]{1,2,0:T(8,128)S(1)} %get-tuple-element.15), channel_id=1, source_target_pairs={{0,3},{1,2},{2,1},{3,0},{4,7},{5,6},{6,5},{7,4},{8,11},{9,10},{10,... | collective-permute-start | bytes 1572872 | tf_op jit(solution)/shard_map/ppermute | solution.py:96
